TPU v7x, 256 devices: a whole 4x4x8 slice. The times are simulated.
256 devices in a mesh: group: 8 (over y, core), dev: 32 (over x, z).
Axes of the slice: x: 4, y: 4, z: 8, core: 2. Of those that a mesh axis runs over, the one named last changes fastest.
Arguments:
- embeddings: bfloat16 [262144, 768], P(('group', 'dev')), may hold values from -6 to 6
- cluster_ids: int32 [1024], P(('group', 'dev')), may hold values from 0 to 1023, as said below
Outputs:
- nearest: float32 [262144], P(('group', 'dev'))
Inputs may be any that keep to these rules, and one draw needn't show every extreme that they name: `cluster_ids`: each cluster is a run of 1 to 29 consecutive blocks inside one cluster group of 128 blocks (a group's first block starts a cluster, its last block is a cluster of one block), and its id is the index of its first block; some cluster of every group has exactly 29 blocks.
All inputs are finite; a program needn't handle non-finite values.
Results may differ from a plain program's by a relative error of at most 0.0012.
Values may be sent and summed in bfloat16 or wider, within the bound.
No kernel may reach another device: no remote copies, remote signals or barrier semaphores. Data moves between devices by JAX's collectives and lax.ppermute only.
A program may use at most 192 MiB of HBM per device.

v0:
```python
import jax
import jax.numpy as jnp
from jax import lax
from jax.sharding import PartitionSpec as P


def from_behind(value, axis, steps):
    count = lax.axis_size(axis)
    initial, last = (max(0, -steps), min(count, count - steps))
    return lax.ppermute(value, axis, [(source, source + steps) for source in range(initial, last)])


def unit_rows(embeddings):
    values_f = embeddings.astype(jnp.float32)
    squares = jnp.sum(values_f * values_f, axis=1, keepdims=True)
    return (values_f * lax.rsqrt(squares + 1e-06)).astype(jnp.bfloat16)


def body(embeddings, cluster_ids):
    rows = embeddings.shape[0]
    blocks = cluster_ids.shape[0]
    width = rows // blocks
    count = lax.axis_size("dev")
    span = count // 4
    place = lax.axis_index("dev")
    unit = unit_rows(embeddings)
    own_tags = cluster_ids + 1
    row_tags = jnp.repeat(own_tags, width)
    local = jnp.arange(rows, dtype=jnp.int32)
    scores = jnp.dot(unit, unit.T, preferred_element_type=jnp.float32)
    keep = (row_tags[:, None] == row_tags[None, :]) & (local[:, None] != local[None, :])
    best = jnp.max(jnp.where(keep, scores + 2.0, jnp.zeros_like(scores)), axis=1)
    column_list = [jnp.zeros((rows,), jnp.float32)]
    current = unit
    current_tags = own_tags
    for offset in range(1, span):
        current, current_tags = from_behind((current, current_tags), "dev", -1)
        partner = current
        partner_tags = current_tags
        matched = jnp.any(own_tags[:, None] == partner_tags[None, :])

        def tile(unused):
            sims = jnp.dot(unit, partner.T, preferred_element_type=jnp.float32)
            partner_rows = jnp.repeat(partner_tags, width)
            shifted = jnp.where(
                row_tags[:, None] == partner_rows[None, :], sims + 2.0, jnp.zeros_like(sims)
            )
            return (jnp.max(shifted, axis=1), jnp.max(shifted, axis=0))

        def skipped(unused):
            empty = jnp.zeros((rows,), jnp.float32)
            return (empty, empty)

        row_part, column_part = lax.cond(matched, tile, skipped, 0)
        best = jnp.maximum(best, row_part)
        column_list.append(column_part)
    columns = jnp.stack(column_list, axis=0)
    table = jnp.zeros((count + span, rows), jnp.float32)
    table = lax.dynamic_update_slice(table, columns, (place, jnp.int32(0)))
    table = lax.pmax(table[:count], "dev")
    best = jnp.maximum(best, lax.dynamic_index_in_dim(table, place, 0, keepdims=False))
    return best - 2.0


def solution(mesh):
    return jax.shard_map(
        body,
        mesh=mesh,
        in_specs=(P(("group", "dev"), None), P(("group", "dev"))),
        out_specs=P(("group", "dev")),
        check_vma=False,
    )
```

profile of v0, /device:TPU:4, one launch (start us, length us, event | category | flops | bytes accessed | tf_op | source)
XLA Modules:
  0.0 497.3 jit_solution(11326214204801013188)
XLA Ops:
  6.5 1.9 fusion.15
  8.5 0.3 fusion.16
  8.8 7.7 %collective-permute-start.1 = (bf16[1024,768]{1,0:T(8,128)(2,1)S(1)}, bf16[1024,768]{1,0:T(8,128)(2,1)S(1)}, u32[]{:S(2)}, u32[]{:S(2)}) collective-permute-start(bf16[1024,768]{1,0:T(8,128)(2,1)S(1)} %fusion.16), channel_id=1, source_target_pairs={{1,0},{2,1},{3,2},{4,3},{5,4},{6,5},{7,6},{8,7},{9,8},{10,9},{11,1... | collective-permute-start | bytes 4718600 | tf_op jit(solution)/shard_map/ppermute | solution.py:10
  16.6 33.6 %collective-permute-done.1 = bf16[1024,768]{1,0:T(8,128)(2,1)S(1)} collective-permute-done((bf16[1024,768]{1,0:T(8,128)(2,1)S(1)}, bf16[1024,768]{1,0:T(8,128)(2,1)S(1)}, u32[]{:S(2)}, u32[]{:S(2)}) %collective-permute-start.1) | collective-permute-done | bytes 1572896 | tf_op jit(solution)/shard_map/ppermute | solution.py:10
  50.2 6.5 %collective-permute-start.3 = (bf16[1024,768]{1,0:T(8,128)(2,1)S(1)}, bf16[1024,768]{1,0:T(8,128)(2,1)S(1)}, u32[]{:S(2)}, u32[]{:S(2)}) collective-permute-start(bf16[1024,768]{1,0:T(8,128)(2,1)S(1)} %collective-permute-done.1), channel_id=1, source_target_pairs={{1,0},{2,1},{3,2},{4,3},{5,4},{6,5},{7,6},{8,7},{9,8},{10,9},{11,1... | collective-permute-start | bytes 4718600 | tf_op jit(solution)/shard_map/ppermute | solution.py:10
  56.7 32.8 %collective-permute-done.3 = bf16[1024,768]{1,0:T(8,128)(2,1)S(1)} collective-permute-done((bf16[1024,768]{1,0:T(8,128)(2,1)S(1)}, bf16[1024,768]{1,0:T(8,128)(2,1)S(1)}, u32[]{:S(2)}, u32[]{:S(2)}) %collective-permute-start.3) | collective-permute-done | bytes 1572896 | tf_op jit(solution)/shard_map/ppermute | solution.py:10
  89.5 6.5 %collective-permute-start.5 = (bf16[1024,768]{1,0:T(8,128)(2,1)S(1)}, bf16[1024,768]{1,0:T(8,128)(2,1)S(1)}, u32[]{:S(2)}, u32[]{:S(2)}) collective-permute-start(bf16[1024,768]{1,0:T(8,128)(2,1)S(1)} %collective-permute-done.3), channel_id=1, source_target_pairs={{1,0},{2,1},{3,2},{4,3},{5,4},{6,5},{7,6},{8,7},{9,8},{10,9},{11,1... | collective-permute-start | bytes 4718600 | tf_op jit(solution)/shard_map/ppermute | solution.py:10
  96.0 31.9 %collective-permute-done.5 = bf16[1024,768]{1,0:T(8,128)(2,1)S(1)} collective-permute-done((bf16[1024,768]{1,0:T(8,128)(2,1)S(1)}, bf16[1024,768]{1,0:T(8,128)(2,1)S(1)}, u32[]{:S(2)}, u32[]{:S(2)}) %collective-permute-start.5) | collective-permute-done | bytes 1572896 | tf_op jit(solution)/shard_map/ppermute | solution.py:10
  127.9 6.5 %collective-permute-start.7 = (bf16[1024,768]{1,0:T(8,128)(2,1)S(1)}, bf16[1024,768]{1,0:T(8,128)(2,1)S(1)}, u32[]{:S(2)}, u32[]{:S(2)}) collective-permute-start(bf16[1024,768]{1,0:T(8,128)(2,1)S(1)} %collective-permute-done.5), channel_id=1, source_target_pairs={{1,0},{2,1},{3,2},{4,3},{5,4},{6,5},{7,6},{8,7},{9,8},{10,9},{11,1... | collective-permute-start | bytes 4718600 | tf_op jit(solution)/shard_map/ppermute | solution.py:10
  134.4 31.1 %collective-permute-done.7 = bf16[1024,768]{1,0:T(8,128)(2,1)S(1)} collective-permute-done((bf16[1024,768]{1,0:T(8,128)(2,1)S(1)}, bf16[1024,768]{1,0:T(8,128)(2,1)S(1)}, u32[]{:S(2)}, u32[]{:S(2)}) %collective-permute-start.7) | collective-permute-done | bytes 1572896 | tf_op jit(solution)/shard_map/ppermute | solution.py:10
  165.4 6.5 %collective-permute-start.9 = (bf16[1024,768]{1,0:T(8,128)(2,1)S(1)}, bf16[1024,768]{1,0:T(8,128)(2,1)S(1)}, u32[]{:S(2)}, u32[]{:S(2)}) collective-permute-start(bf16[1024,768]{1,0:T(8,128)(2,1)S(1)} %collective-permute-done.7), channel_id=1, source_target_pairs={{1,0},{2,1},{3,2},{4,3},{5,4},{6,5},{7,6},{8,7},{9,8},{10,9},{11,1... | collective-permute-start | bytes 4718600 | tf_op jit(solution)/shard_map/ppermute | solution.py:10
  171.9 30.2 %collective-permute-done.9 = bf16[1024,768]{1,0:T(8,128)(2,1)S(1)} collective-permute-done((bf16[1024,768]{1,0:T(8,128)(2,1)S(1)}, bf16[1024,768]{1,0:T(8,128)(2,1)S(1)}, u32[]{:S(2)}, u32[]{:S(2)}) %collective-permute-start.9) | collective-permute-done | bytes 1572896 | tf_op jit(solution)/shard_map/ppermute | solution.py:10
  202.1 6.5 %collective-permute-start.11 = (bf16[1024,768]{1,0:T(8,128)(2,1)S(1)}, bf16[1024,768]{1,0:T(8,128)(2,1)}, u32[]{:S(2)}, u32[]{:S(2)}) collective-permute-start(bf16[1024,768]{1,0:T(8,128)(2,1)S(1)} %collective-permute-done.9), channel_id=1, source_target_pairs={{1,0},{2,1},{3,2},{4,3},{5,4},{6,5},{7,6},{8,7},{9,8},{10,9},{11,1... | collective-permute-start | bytes 4718600 | tf_op jit(solution)/shard_map/ppermute | solution.py:10
  208.6 29.3 %collective-permute-done.11 = bf16[1024,768]{1,0:T(8,128)(2,1)} collective-permute-done((bf16[1024,768]{1,0:T(8,128)(2,1)S(1)}, bf16[1024,768]{1,0:T(8,128)(2,1)}, u32[]{:S(2)}, u32[]{:S(2)}) %collective-permute-start.11) | collective-permute-done | bytes 1572896 | tf_op jit(solution)/shard_map/ppermute | solution.py:10
  238.0 6.6 %collective-permute-start.13 = (bf16[1024,768]{1,0:T(8,128)(2,1)}, bf16[1024,768]{1,0:T(8,128)(2,1)S(1)}, u32[]{:S(2)}, u32[]{:S(2)}) collective-permute-start(bf16[1024,768]{1,0:T(8,128)(2,1)} %collective-permute-done.11), channel_id=1, source_target_pairs={{1,0},{2,1},{3,2},{4,3},{5,4},{6,5},{7,6},{8,7},{9,8},{10,9},{11,1... | collective-permute-start | bytes 4718600 | tf_op jit(solution)/shard_map/ppermute | solution.py:10
  244.6 1.9 collective-permute-start
  246.5 0.1 broadcast_bitcast_fusion.7
  246.6 26.8 %collective-permute-done = s32[4]{0:T(128)S(1)} collective-permute-done((s32[4]{0:T(128)S(1)}, s32[4]{0:T(128)S(1)}, u32[]{:S(2)}, u32[]{:S(2)}) %collective-permute-start) | collective-permute-done | bytes 48 | tf_op jit(solution)/shard_map/ppermute | solution.py:10
  273.4 6.5 %collective-permute-start.2 = (s32[4]{0:T(128)S(1)}, s32[4]{0:T(128)S(1)}, u32[]{:S(2)}, u32[]{:S(2)}) collective-permute-start(s32[4]{0:T(128)S(1)} %collective-permute-done), channel_id=1, source_target_pairs={{1,0},{2,1},{3,2},{4,3},{5,4},{6,5},{7,6},{8,7},{9,8},{10,9},{11,1... | collective-permute-start | bytes 56 | tf_op jit(solution)/shard_map/ppermute | solution.py:10
  279.9 1.3 collective-permute-done.2
  281.2 6.3 %collective-permute-start.4 = (s32[4]{0:T(128)S(1)}, s32[4]{0:T(128)S(1)}, u32[]{:S(2)}, u32[]{:S(2)}) collective-permute-start(s32[4]{0:T(128)S(1)} %collective-permute-done.2), channel_id=1, source_target_pairs={{1,0},{2,1},{3,2},{4,3},{5,4},{6,5},{7,6},{8,7},{9,8},{10,9},{11,1... | collective-permute-start | bytes 56 | tf_op jit(solution)/shard_map/ppermute | solution.py:10
  287.5 1.3 collective-permute-done.4
  288.7 6.3 %collective-permute-start.6 = (s32[4]{0:T(128)S(1)}, s32[4]{0:T(128)S(1)}, u32[]{:S(2)}, u32[]{:S(2)}) collective-permute-start(s32[4]{0:T(128)S(1)} %collective-permute-done.4), channel_id=1, source_target_pairs={{1,0},{2,1},{3,2},{4,3},{5,4},{6,5},{7,6},{8,7},{9,8},{10,9},{11,1... | collective-permute-start | bytes 56 | tf_op jit(solution)/shard_map/ppermute | solution.py:10
  295.0 1.3 collective-permute-done.6
  296.3 6.3 %collective-permute-start.8 = (s32[4]{0:T(128)S(1)}, s32[4]{0:T(128)S(1)}, u32[]{:S(2)}, u32[]{:S(2)}) collective-permute-start(s32[4]{0:T(128)S(1)} %collective-permute-done.6), channel_id=1, source_target_pairs={{1,0},{2,1},{3,2},{4,3},{5,4},{6,5},{7,6},{8,7},{9,8},{10,9},{11,1... | collective-permute-start | bytes 56 | tf_op jit(solution)/shard_map/ppermute | solution.py:10
  302.6 1.3 collective-permute-done.8
  303.8 6.3 %collective-permute-start.10 = (s32[4]{0:T(128)S(1)}, s32[4]{0:T(128)S(1)}, u32[]{:S(2)}, u32[]{:S(2)}) collective-permute-start(s32[4]{0:T(128)S(1)} %collective-permute-done.8), channel_id=1, source_target_pairs={{1,0},{2,1},{3,2},{4,3},{5,4},{6,5},{7,6},{8,7},{9,8},{10,9},{11,1... | collective-permute-start | bytes 56 | tf_op jit(solution)/shard_map/ppermute | solution.py:10
  310.1 1.3 collective-permute-done.10
  311.4 6.3 %collective-permute-start.12 = (s32[4]{0:T(128)S(1)}, s32[4]{0:T(128)S(1)}, u32[]{:S(2)}, u32[]{:S(2)}) collective-permute-start(s32[4]{0:T(128)S(1)} %collective-permute-done.10), channel_id=1, source_target_pairs={{1,0},{2,1},{3,2},{4,3},{5,4},{6,5},{7,6},{8,7},{9,8},{10,9},{11,1... | collective-permute-start | bytes 56 | tf_op jit(solution)/shard_map/ppermute | solution.py:10
  317.7 1.3 collective-permute-done.12
  319.0 0.9 compare_reduce_fusion
  324.3 0.1 broadcast_in_dim.22
  324.4 3.5 conditional.7
  324.4 3.4 fusion
  327.8 3.5 conditional.8
  327.9 0.1 broadcast_bitcast_fusion.1
  328.0 3.4 fusion.2
  331.4 3.5 conditional.9
  331.5 3.4 fusion.4
  334.9 3.5 conditional.10
  335.0 3.4 fusion.6
  338.5 0.2 conditional.13
  338.8 0.3 dynamic_update_slice.3
  339.1 0.7 slice.4
  339.8 2.1 select_reduce_fusion
  341.9 147.2 %all-reduce.2.cloned.1.call-done = f32[32,1024]{1,0:T(8,128)} async-done(((f32[32,1024]{1,0:T(8,128)}), f32[32,1024]{1,0:T(8,128)}) %all-reduce.2.cloned.1.call-update) | async-done | bytes 131088 | tf_op jit(solution)/shard_map/pmax | solution.py:60
  489.1 0.8 constant_dynamic-slice_fusion
  489.8 0.6 maximum_add_fusion
  (42 shorter events, 0.5 us)
Async XLA Ops:
  6.5 1.9 copy-start
  6.5 482.5 %all-reduce.2.cloned.1.call-start = ((), (), s32[]{:S(2)}) async-start(), calls=%async_computation | async-start | bytes 262144 | tf_op jit(solution)/shard_map/pmax | solution.py:60
  8.5 236.1 %copy-start.6 = (s32[4]{0:T(128)S(1)}, s32[4]{0:T(128)}, u32[]{:S(2)}) copy-start(s32[4]{0:T(128)} %param.17) | copy-start | bytes 52
  8.8 41.4 %collective-permute-start.1 = (bf16[1024,768]{1,0:T(8,128)(2,1)S(1)}, bf16[1024,768]{1,0:T(8,128)(2,1)S(1)}, u32[]{:S(2)}, u32[]{:S(2)}) collective-permute-start(bf16[1024,768]{1,0:T(8,128)(2,1)S(1)} %fusion.16), channel_id=1, source_target_pairs={{1,0},{2,1},{3,2},{4,3},{5,4},{6,5},{7,6},{8,7},{9,8},{10,9},{11,1... | collective-permute-start | bytes 4718600 | tf_op jit(solution)/shard_map/ppermute | solution.py:10
  50.2 6.5 %copy-start.5 = (bf16[1024,768]{1,0:T(8,128)(2,1)}, bf16[1024,768]{1,0:T(8,128)(2,1)S(1)}, u32[]{:S(2)}) copy-start(bf16[1024,768]{1,0:T(8,128)(2,1)S(1)} %collective-permute-done.1) | copy-start | bytes 4718596
  50.2 39.3 %collective-permute-start.3 = (bf16[1024,768]{1,0:T(8,128)(2,1)S(1)}, bf16[1024,768]{1,0:T(8,128)(2,1)S(1)}, u32[]{:S(2)}, u32[]{:S(2)}) collective-permute-start(bf16[1024,768]{1,0:T(8,128)(2,1)S(1)} %collective-permute-done.1), channel_id=1, source_target_pairs={{1,0},{2,1},{3,2},{4,3},{5,4},{6,5},{7,6},{8,7},{9,8},{10,9},{11,1... | collective-permute-start | bytes 4718600 | tf_op jit(solution)/shard_map/ppermute | solution.py:10
  89.5 6.5 %copy-start.4 = (bf16[1024,768]{1,0:T(8,128)(2,1)}, bf16[1024,768]{1,0:T(8,128)(2,1)S(1)}, u32[]{:S(2)}) copy-start(bf16[1024,768]{1,0:T(8,128)(2,1)S(1)} %collective-permute-done.3) | copy-start | bytes 4718596
  89.5 38.4 %collective-permute-start.5 = (bf16[1024,768]{1,0:T(8,128)(2,1)S(1)}, bf16[1024,768]{1,0:T(8,128)(2,1)S(1)}, u32[]{:S(2)}, u32[]{:S(2)}) collective-permute-start(bf16[1024,768]{1,0:T(8,128)(2,1)S(1)} %collective-permute-done.3), channel_id=1, source_target_pairs={{1,0},{2,1},{3,2},{4,3},{5,4},{6,5},{7,6},{8,7},{9,8},{10,9},{11,1... | collective-permute-start | bytes 4718600 | tf_op jit(solution)/shard_map/ppermute | solution.py:10
  127.9 6.5 %copy-start.3 = (bf16[1024,768]{1,0:T(8,128)(2,1)}, bf16[1024,768]{1,0:T(8,128)(2,1)S(1)}, u32[]{:S(2)}) copy-start(bf16[1024,768]{1,0:T(8,128)(2,1)S(1)} %collective-permute-done.5) | copy-start | bytes 4718596
  127.9 37.6 %collective-permute-start.7 = (bf16[1024,768]{1,0:T(8,128)(2,1)S(1)}, bf16[1024,768]{1,0:T(8,128)(2,1)S(1)}, u32[]{:S(2)}, u32[]{:S(2)}) collective-permute-start(bf16[1024,768]{1,0:T(8,128)(2,1)S(1)} %collective-permute-done.5), channel_id=1, source_target_pairs={{1,0},{2,1},{3,2},{4,3},{5,4},{6,5},{7,6},{8,7},{9,8},{10,9},{11,1... | collective-permute-start | bytes 4718600 | tf_op jit(solution)/shard_map/ppermute | solution.py:10
  165.4 72.6 %copy-start.2 = (bf16[1024,768]{1,0:T(8,128)(2,1)}, bf16[1024,768]{1,0:T(8,128)(2,1)S(1)}, u32[]{:S(2)}) copy-start(bf16[1024,768]{1,0:T(8,128)(2,1)S(1)} %collective-permute-done.7) | copy-start | bytes 4718596
  165.4 36.7 %collective-permute-start.9 = (bf16[1024,768]{1,0:T(8,128)(2,1)S(1)}, bf16[1024,768]{1,0:T(8,128)(2,1)S(1)}, u32[]{:S(2)}, u32[]{:S(2)}) collective-permute-start(bf16[1024,768]{1,0:T(8,128)(2,1)S(1)} %collective-permute-done.7), channel_id=1, source_target_pairs={{1,0},{2,1},{3,2},{4,3},{5,4},{6,5},{7,6},{8,7},{9,8},{10,9},{11,1... | collective-permute-start | bytes 4718600 | tf_op jit(solution)/shard_map/ppermute | solution.py:10
  202.1 6.5 %copy-start.1 = (bf16[1024,768]{1,0:T(8,128)(2,1)}, bf16[1024,768]{1,0:T(8,128)(2,1)S(1)}, u32[]{:S(2)}) copy-start(bf16[1024,768]{1,0:T(8,128)(2,1)S(1)} %collective-permute-done.9) | copy-start | bytes 4718596
  202.1 35.8 %collective-permute-start.11 = (bf16[1024,768]{1,0:T(8,128)(2,1)S(1)}, bf16[1024,768]{1,0:T(8,128)(2,1)}, u32[]{:S(2)}, u32[]{:S(2)}) collective-permute-start(bf16[1024,768]{1,0:T(8,128)(2,1)S(1)} %collective-permute-done.9), channel_id=1, source_target_pairs={{1,0},{2,1},{3,2},{4,3},{5,4},{6,5},{7,6},{8,7},{9,8},{10,9},{11,1... | collective-permute-start | bytes 4718600 | tf_op jit(solution)/shard_map/ppermute | solution.py:10
  238.0 100.5 %collective-permute-start.13 = (bf16[1024,768]{1,0:T(8,128)(2,1)}, bf16[1024,768]{1,0:T(8,128)(2,1)S(1)}, u32[]{:S(2)}, u32[]{:S(2)}) collective-permute-start(bf16[1024,768]{1,0:T(8,128)(2,1)} %collective-permute-done.11), channel_id=1, source_target_pairs={{1,0},{2,1},{3,2},{4,3},{5,4},{6,5},{7,6},{8,7},{9,8},{10,9},{11,1... | collective-permute-start | bytes 4718600 | tf_op jit(solution)/shard_map/ppermute | solution.py:10
  244.6 28.8 %collective-permute-start = (s32[4]{0:T(128)S(1)}, s32[4]{0:T(128)S(1)}, u32[]{:S(2)}, u32[]{:S(2)}) collective-permute-start(s32[4]{0:T(128)S(1)} %broadcast_add_fusion), channel_id=1, source_target_pairs={{1,0},{2,1},{3,2},{4,3},{5,4},{6,5},{7,6},{8,7},{9,8},{10,9},{11,1... | collective-permute-start | bytes 56 | tf_op jit(solution)/shard_map/ppermute | solution.py:10
  273.4 7.8 %collective-permute-start.2 = (s32[4]{0:T(128)S(1)}, s32[4]{0:T(128)S(1)}, u32[]{:S(2)}, u32[]{:S(2)}) collective-permute-start(s32[4]{0:T(128)S(1)} %collective-permute-done), channel_id=1, source_target_pairs={{1,0},{2,1},{3,2},{4,3},{5,4},{6,5},{7,6},{8,7},{9,8},{10,9},{11,1... | collective-permute-start | bytes 56 | tf_op jit(solution)/shard_map/ppermute | solution.py:10
  281.2 7.6 %collective-permute-start.4 = (s32[4]{0:T(128)S(1)}, s32[4]{0:T(128)S(1)}, u32[]{:S(2)}, u32[]{:S(2)}) collective-permute-start(s32[4]{0:T(128)S(1)} %collective-permute-done.2), channel_id=1, source_target_pairs={{1,0},{2,1},{3,2},{4,3},{5,4},{6,5},{7,6},{8,7},{9,8},{10,9},{11,1... | collective-permute-start | bytes 56 | tf_op jit(solution)/shard_map/ppermute | solution.py:10
  288.7 7.6 %collective-permute-start.6 = (s32[4]{0:T(128)S(1)}, s32[4]{0:T(128)S(1)}, u32[]{:S(2)}, u32[]{:S(2)}) collective-permute-start(s32[4]{0:T(128)S(1)} %collective-permute-done.4), channel_id=1, source_target_pairs={{1,0},{2,1},{3,2},{4,3},{5,4},{6,5},{7,6},{8,7},{9,8},{10,9},{11,1... | collective-permute-start | bytes 56 | tf_op jit(solution)/shard_map/ppermute | solution.py:10
  296.3 7.6 %collective-permute-start.8 = (s32[4]{0:T(128)S(1)}, s32[4]{0:T(128)S(1)}, u32[]{:S(2)}, u32[]{:S(2)}) collective-permute-start(s32[4]{0:T(128)S(1)} %collective-permute-done.6), channel_id=1, source_target_pairs={{1,0},{2,1},{3,2},{4,3},{5,4},{6,5},{7,6},{8,7},{9,8},{10,9},{11,1... | collective-permute-start | bytes 56 | tf_op jit(solution)/shard_map/ppermute | solution.py:10
  303.8 7.6 %collective-permute-start.10 = (s32[4]{0:T(128)S(1)}, s32[4]{0:T(128)S(1)}, u32[]{:S(2)}, u32[]{:S(2)}) collective-permute-start(s32[4]{0:T(128)S(1)} %collective-permute-done.8), channel_id=1, source_target_pairs={{1,0},{2,1},{3,2},{4,3},{5,4},{6,5},{7,6},{8,7},{9,8},{10,9},{11,1... | collective-permute-start | bytes 56 | tf_op jit(solution)/shard_map/ppermute | solution.py:10
  311.4 7.6 %collective-permute-start.12 = (s32[4]{0:T(128)S(1)}, s32[4]{0:T(128)S(1)}, u32[]{:S(2)}, u32[]{:S(2)}) collective-permute-start(s32[4]{0:T(128)S(1)} %collective-permute-done.10), channel_id=1, source_target_pairs={{1,0},{2,1},{3,2},{4,3},{5,4},{6,5},{7,6},{8,7},{9,8},{10,9},{11,1... | collective-permute-start | bytes 56 | tf_op jit(solution)/shard_map/ppermute | solution.py:10
Sparse Core Ops, SparseCore 0:
  339.9 149.0 all-reduce.1
where the time goes:
time: 498 us; the launch traced here: 497 us
  waiting for transfers between devices  371 us (74%)
  starting transfers between devices  86.6 us (17%)
  between operations  18.1 us (4%)
  matrix products  15.7 us (3%)
    ppermute x14, waiting for transfers between devices, from_behind(): lax.ppermute(value, axis, [(source, source + steps) for source in range(i...  223 us
    pmax x1, waiting for transfers between devices, body(): table = lax.pmax(table[:count], 'dev')  147 us
    ppermute x14, starting transfers between devices, from_behind(): lax.ppermute(value, axis, [(source, source + steps) for source in range(i...  86.6 us
    dot_general x4, matrix products, tile(): sims = jnp.dot(unit, partner.T, preferred_element_type=jnp.float32)  13.6 us
  transfers between devices with their start and end apart: 15, of which 14 were waited for; matrix products, arithmetic and copies ran while one was open for 3% of the time, Pallas kernels for 0%

commit v1 on v0

v1 whole, which is shorter than its diff:
```python
import jax
import jax.numpy as jnp
from jax import lax
from jax.sharding import PartitionSpec as P


def from_behind(value, axis, steps):
    count = lax.axis_size(axis)
    initial, last = (max(0, -steps), min(count, count - steps))
    return lax.ppermute(value, axis, [(source, source + steps) for source in range(initial, last)])


def unit_rows(embeddings):
    values_f = embeddings.astype(jnp.float32)
    squares = jnp.sum(values_f * values_f, axis=1, keepdims=True)
    return (values_f * lax.rsqrt(squares + 1e-06)).astype(jnp.bfloat16)


def body(embeddings, cluster_ids):
    rows = embeddings.shape[0]
    blocks = cluster_ids.shape[0]
    width = rows // blocks
    count = lax.axis_size("dev")
    reach = count // 4
    place = lax.axis_index("dev")
    unit = unit_rows(embeddings)
    all_tags = lax.all_gather(cluster_ids, "dev", tiled=True) + 1

    def tags_at(offset, sentinel):
        index = place + offset
        valid = (index >= 0) & (index < count)
        start = jnp.clip(index, 0, count - 1) * blocks
        tags = lax.dynamic_slice_in_dim(all_tags, start, blocks, 0)
        return jnp.repeat(jnp.where(valid, tags, sentinel), width)

    def tile(a, a_tags, b, b_tags):
        sims = jnp.dot(a, b.T, preferred_element_type=jnp.float32)
        shifted = jnp.where(a_tags[:, None] == b_tags[None, :], sims + 2.0, jnp.zeros_like(sims))
        return jnp.max(shifted, axis=1), jnp.max(shifted, axis=0)

    own_tags = jnp.repeat(cluster_ids + 1, width)
    local = jnp.arange(rows, dtype=jnp.int32)
    scores = jnp.dot(unit, unit.T, preferred_element_type=jnp.float32)
    keep = (own_tags[:, None] == own_tags[None, :]) & (local[:, None] != local[None, :])
    best = jnp.max(jnp.where(keep, scores + 2.0, jnp.zeros_like(scores)), axis=1)

    ahead_steps = reach // 2
    behind_steps = (reach - 1) // 2
    ahead = [unit]
    for step in range(ahead_steps):
        ahead.append(from_behind(ahead[-1], "dev", -1))
    behind = [unit]
    for step in range(behind_steps):
        behind.append(from_behind(behind[-1], "dev", 1))
    ahead_tags = [own_tags] + [tags_at(j, -2) for j in range(1, ahead_steps + 1)]
    behind_tags = [own_tags] + [tags_at(-i, -1) for i in range(1, behind_steps + 1)]

    to_ahead = [None] * (ahead_steps + 1)
    to_behind = [None] * (behind_steps + 1)
    for k in range(1, reach):
        i, j = k // 2, k - k // 2
        row_part, column_part = tile(behind[i], behind_tags[i], ahead[j], ahead_tags[j])
        if i == 0:
            best = jnp.maximum(best, row_part)
        else:
            to_behind[i] = row_part if to_behind[i] is None else jnp.maximum(to_behind[i], row_part)
        to_ahead[j] = column_part if to_ahead[j] is None else jnp.maximum(to_ahead[j], column_part)

    for i in range(1, behind_steps + 1):
        best = jnp.maximum(best, from_behind(to_behind[i], "dev", -i))
    for j in range(1, ahead_steps + 1):
        best = jnp.maximum(best, from_behind(to_ahead[j], "dev", j))
    return best - 2.0


def solution(mesh):
    return jax.shard_map(
        body,
        mesh=mesh,
        in_specs=(P(("group", "dev"), None), P(("group", "dev"))),
        out_specs=P(("group", "dev")),
        check_vma=False,
    )
```

time: 498 us -> 219 us (0.44)
  waiting for transfers between devices: 371 us -> 73.6 us
  blocking collectives: 0 us -> 44.7 us
  starting transfers between devices: 86.6 us -> 61.1 us
  matrix products: 15.7 us -> 33.2 us
  between operations: 18.1 us -> 1.01 us
    ppermute x14, waiting for transfers between devices: 223 us -> 73.6 us  [from_behind(): lax.ppermute(value, axis, [(source, source + steps) for source in range(i...]
    pmax x1 -> x0, waiting for transfers between devices: 147 us -> none  [body(): table = lax.pmax(table[:count], 'dev')]
    unnamed x0 -> x1, blocking collectives: none -> 44.7 us
    ppermute x14, starting transfers between devices: 86.6 us -> 61.1 us  [from_behind(): lax.ppermute(value, axis, [(source, source + steps) for source in range(i...]
    dot_general x4 -> x7, matrix products: 13.6 us -> 31.1 us  [tile(): sims = jnp.dot(a, b.T, preferred_element_type=jnp.float32)]
  transfers between devices with their start and end apart: 15 -> 14, of which waited for: 14 -> 6; matrix products, arithmetic and copies ran while one was open for 3% -> 12% of each run, Pallas kernels for 0% -> 0%
where the time goes in v1:
time: 219 us; the launch traced here: 218 us
  waiting for transfers between devices  73.6 us (34%)
  starting transfers between devices  61.1 us (28%)
  blocking collectives  44.7 us (20%)
  matrix products  33.2 us (15%)
  other arithmetic  2.97 us (1%)
    ppermute x14, waiting for transfers between devices, from_behind(): lax.ppermute(value, axis, [(source, source + steps) for source in range(i...  73.6 us
    ppermute x14, starting transfers between devices, from_behind(): lax.ppermute(value, axis, [(source, source + steps) for source in range(i...  61.1 us
    unnamed x1, blocking collectives  44.7 us
    dot_general x7, matrix products, tile(): sims = jnp.dot(a, b.T, preferred_element_type=jnp.float32)  31.1 us
  transfers between devices with their start and end apart: 14, of which 6 were waited for; matrix products, arithmetic and copies ran while one was open for 12% of the time, Pallas kernels for 0%

profile of v1, /device:TPU:4, one launch (start us, length us, event | category | flops | bytes accessed | tf_op | source)
XLA Modules:
  0.0 217.8 jit_solution(16593346139339233840)
XLA Ops:
  0.0 1.9 fusion.15
  1.9 0.0 copy-start.2
  1.9 0.0 copy-start.1
  2.0 0.3 fusion.16
  2.3 7.7 %collective-permute-start = (bf16[1024,768]{1,0:T(8,128)(2,1)S(1)}, bf16[1024,768]{1,0:T(8,128)(2,1)}, u32[]{:S(2)}, u32[]{:S(2)}) collective-permute-start(bf16[1024,768]{1,0:T(8,128)(2,1)S(1)} %fusion.16), channel_id=1, source_target_pairs={{1,0},{2,1},{3,2},{4,3},{5,4},{6,5},{7,6},{8,7},{9,8},{10,9},{11,1... | collective-permute-start | bytes 4718600 | tf_op jit(solution)/shard_map/ppermute | solution.py:10
  10.0 1.9 collective-permute-start.1
  12.0 31.7 %collective-permute-done = bf16[1024,768]{1,0:T(8,128)(2,1)} collective-permute-done((bf16[1024,768]{1,0:T(8,128)(2,1)S(1)}, bf16[1024,768]{1,0:T(8,128)(2,1)}, u32[]{:S(2)}, u32[]{:S(2)}) %collective-permute-start) | collective-permute-done | bytes 1572896 | tf_op jit(solution)/shard_map/ppermute | solution.py:10
  43.7 6.6 %collective-permute-start.2 = (bf16[1024,768]{1,0:T(8,128)(2,1)}, bf16[1024,768]{1,0:T(8,128)(2,1)}, u32[]{:S(2)}, u32[]{:S(2)}) collective-permute-start(bf16[1024,768]{1,0:T(8,128)(2,1)} %collective-permute-done), channel_id=1, source_target_pairs={{1,0},{2,1},{3,2},{4,3},{5,4},{6,5},{7,6},{8,7},{9,8},{10,9},{11,1... | collective-permute-start | bytes 4718600 | tf_op jit(solution)/shard_map/ppermute | solution.py:10
  50.3 0.6 dynamic-slice
  51.6 0.2 dynamic-update-slice
  51.8 44.7 %all-reduce = s32[128]{0:T(128)S(1)} all-reduce(s32[128]{0:T(128)S(1)} %dynamic-update-slice), channel_id=1, replica_groups=mesh['group'=8,'dev'=32] {'dev'}, use_global_device_ids=true, to_apply=%add | all-reduce | flops 128 | bytes 1024
  96.5 0.0 collective-permute-done.1
  96.5 1.9 collective-permute-start.4
  98.4 0.1 broadcast_select_fusion
  98.5 0.1 broadcast_bitcast_fusion.7
  98.6 0.0 collective-permute-done.2
  98.6 6.0 %collective-permute-start.5 = (bf16[1024,768]{1,0:T(8,128)(2,1)}, bf16[1024,768]{1,0:T(8,128)(2,1)S(1)}, u32[]{:S(2)}, u32[]{:S(2)}) collective-permute-start(bf16[1024,768]{1,0:T(8,128)(2,1)} %collective-permute-done.2), channel_id=1, source_target_pairs={{1,0},{2,1},{3,2},{4,3},{5,4},{6,5},{7,6},{8,7},{9,8},{10,9},{11,1... | collective-permute-start | bytes 4718600 | tf_op jit(solution)/shard_map/ppermute | solution.py:10
  104.6 0.1 broadcast_bitcast_fusion.6
  104.7 0.1 broadcast_bitcast_fusion
  104.8 0.1 broadcast_bitcast_fusion.2
  104.9 0.1 broadcast_bitcast_fusion.4
  104.9 3.2 %fusion.17 = f32[1024,1024]{0,1:T(8,128)S(1)} fusion(bf16[1024,768]{1,0:T(8,128)(2,1)S(1)} %fusion.16, bf16[1024,768]{1,0:T(8,128)(2,1)} %collective-permute-done), kind=kOutput, calls=%fused_computation.47 | convolution fusion | flops 1610612736 | bytes 7340032 | tf_op jit(solution)/shard_map/dot_general | solution.py:37
  108.2 23.8 %collective-permute-done.4 = bf16[1024,768]{1,0:T(8,128)(2,1)S(1)} collective-permute-done((bf16[1024,768]{1,0:T(8,128)(2,1)S(1)}, bf16[1024,768]{1,0:T(8,128)(2,1)S(1)}, u32[]{:S(2)}, u32[]{:S(2)}) %collective-permute-start.4) | collective-permute-done | bytes 1572896 | tf_op jit(solution)/shard_map/ppermute | solution.py:10
  131.9 1.9 collective-permute-start.7
  133.9 3.2 %fusion.18 = f32[1024,1024]{0,1:T(8,128)S(1)} fusion(bf16[1024,768]{1,0:T(8,128)(2,1)S(1)} %collective-permute-done.1, bf16[1024,768]{1,0:T(8,128)(2,1)} %collective-permute-done), kind=kOutput, calls=%fused_computation.48 | convolution fusion | flops 1610612736 | bytes 7340032 | tf_op jit(solution)/shard_map/dot_general | solution.py:37
  137.1 0.0 collective-permute-done.5
  137.1 6.0 %collective-permute-start.8 = (bf16[1024,768]{1,0:T(8,128)(2,1)S(1)}, bf16[1024,768]{1,0:T(8,128)(2,1)S(1)}, u32[]{:S(2)}, u32[]{:S(2)}) collective-permute-start(bf16[1024,768]{1,0:T(8,128)(2,1)S(1)} %collective-permute-done.5), channel_id=1, source_target_pairs={{1,0},{2,1},{3,2},{4,3},{5,4},{6,5},{7,6},{8,7},{9,8},{10,9},{11,1... | collective-permute-start | bytes 4718600 | tf_op jit(solution)/shard_map/ppermute | solution.py:10
  143.1 3.2 %fusion.19 = f32[1024,1024]{0,1:T(8,128)S(1)} fusion(bf16[1024,768]{1,0:T(8,128)(2,1)S(1)} %collective-permute-done.1, bf16[1024,768]{1,0:T(8,128)(2,1)} %collective-permute-done.2), kind=kOutput, calls=%fused_computation.49 | convolution fusion | flops 1610612736 | bytes 7340032 | tf_op jit(solution)/shard_map/dot_general | solution.py:37
  146.4 5.2 %fusion.20 = f32[1024,1024]{0,1:T(8,128)} fusion(bf16[1024,768]{1,0:T(8,128)(2,1)S(1)} %collective-permute-done.4, bf16[1024,768]{1,0:T(8,128)(2,1)} %collective-permute-done.2), kind=kOutput, calls=%fused_computation.50 | convolution fusion | flops 1610612736 | bytes 7340032 | tf_op jit(solution)/shard_map/dot_general | solution.py:37
  151.5 3.8 %fusion.21 = f32[1024,1024]{0,1:T(8,128)} fusion(bf16[1024,768]{1,0:T(8,128)(2,1)S(1)} %collective-permute-done.4, bf16[1024,768]{1,0:T(8,128)(2,1)S(1)} %collective-permute-done.5), kind=kOutput, calls=%fused_computation.51 | convolution fusion | flops 1610612736 | bytes 7340032 | tf_op jit(solution)/shard_map/dot_general | solution.py:37
  155.3 11.2 %collective-permute-done.7 = bf16[1024,768]{1,0:T(8,128)(2,1)S(1)} collective-permute-done((bf16[1024,768]{1,0:T(8,128)(2,1)S(1)}, bf16[1024,768]{1,0:T(8,128)(2,1)S(1)}, u32[]{:S(2)}, u32[]{:S(2)}) %collective-permute-start.7) | collective-permute-done | bytes 1572896 | tf_op jit(solution)/shard_map/ppermute | solution.py:10
  166.5 3.8 %fusion.22 = f32[1024,1024]{0,1:T(8,128)} fusion(bf16[1024,768]{1,0:T(8,128)(2,1)S(1)} %collective-permute-done.7, bf16[1024,768]{1,0:T(8,128)(2,1)S(1)} %collective-permute-done.5), kind=kOutput, calls=%fused_computation.52 | convolution fusion | flops 1610612736 | bytes 7340032 | tf_op jit(solution)/shard_map/dot_general | solution.py:37
  170.3 0.6 collective-permute-done.8
  171.0 8.7 %fusion.2 = (f32[1024]{0:T(1024)S(1)}, f32[1024]{0:T(1024)S(1)}, f32[1024]{0:T(1024)S(1)}, f32[1024]{0:T(1024)S(1)}, f32[1024]{0:T(1024)S(1)}, /*index=5*/f32[10...) fusion(f32[1024,1024]{0,1:T(8,128)S(1)} %fusion.17, ...), kind=kOutput, calls=%fused_computation.13 | convolution fusion | flops 1647298560 | bytes 28401664 | tf_op jit(solution)/shard_map/dot_general | solution.py:37
  179.7 1.9 collective-permute-start.9
  181.6 5.7 %collective-permute-start.12 = (f32[1024]{0:T(1024)S(1)}, f32[1024]{0:T(1024)S(1)}, u32[]{:S(2)}, u32[]{:S(2)}) collective-permute-start(f32[1024]{0:T(1024)S(1)} %max.82), channel_id=1, source_target_pairs={{0,3},{1,4},{2,5},{3,6},{4,7},{5,8},{6,9},{7,10},{8,11},{9,12},{10... | collective-permute-start | bytes 12296 | tf_op jit(solution)/shard_map/ppermute | solution.py:10
  187.4 6.2 %collective-permute-start.6 = (f32[1024]{0:T(1024)S(1)}, f32[1024]{0:T(1024)S(1)}, u32[]{:S(2)}, u32[]{:S(2)}) collective-permute-start(f32[1024]{0:T(1024)S(1)} %max.72), channel_id=1, source_target_pairs={{2,0},{3,1},{4,2},{5,3},{6,4},{7,5},{8,6},{9,7},{10,8},{11,9},{12,... | collective-permute-start | bytes 12296 | tf_op jit(solution)/shard_map/ppermute | solution.py:10
  193.6 1.9 collective-permute-start.11
  195.6 9.3 %collective-permute-start.3 = (f32[1024]{0:T(1024)S(1)}, f32[1024]{0:T(1024)S(1)}, u32[]{:S(2)}, u32[]{:S(2)}) collective-permute-start(f32[1024]{0:T(1024)S(1)} %max.68), channel_id=1, source_target_pairs={{1,0},{2,1},{3,2},{4,3},{5,4},{6,5},{7,6},{8,7},{9,8},{10,9},{11,1... | collective-permute-start | bytes 12296 | tf_op jit(solution)/shard_map/ppermute | solution.py:10
  204.9 0.0 collective-permute-done.9
  204.9 1.9 collective-permute-start.10
  206.8 0.0 collective-permute-done.12
  206.8 1.9 collective-permute-start.13
  208.8 2.0 select_reduce_fusion
  210.8 0.0 collective-permute-done.3
  210.8 1.7 collective-permute-done.10
  212.5 4.6 %collective-permute-done.13 = f32[1024]{0:T(1024)S(1)} collective-permute-done((f32[1024]{0:T(1024)S(1)}, f32[1024]{0:T(1024)S(1)}, u32[]{:S(2)}, u32[]{:S(2)}) %collective-permute-start.13) | collective-permute-done | bytes 4128 | tf_op jit(solution)/shard_map/ppermute | solution.py:10
  217.2 0.6 maximum_add_fusion
  (24 shorter events, 0.1 us)
Async XLA Ops:
  0.0 1.9 copy-start
  1.9 48.4 %copy-start.2 = (u32[256]{0:T(256)S(1)}, u32[256]{0:T(256)}, u32[]{:S(2)}) copy-start(u32[256]{0:T(256)} %constant.43) | copy-start | bytes 3076
  1.9 49.6 %copy-start.1 = (s32[4]{0:T(128)S(1)}, s32[4]{0:T(128)}, u32[]{:S(2)}) copy-start(s32[4]{0:T(128)} %param.3) | copy-start | bytes 52
  2.3 41.4 %collective-permute-start = (bf16[1024,768]{1,0:T(8,128)(2,1)S(1)}, bf16[1024,768]{1,0:T(8,128)(2,1)}, u32[]{:S(2)}, u32[]{:S(2)}) collective-permute-start(bf16[1024,768]{1,0:T(8,128)(2,1)S(1)} %fusion.16), channel_id=1, source_target_pairs={{1,0},{2,1},{3,2},{4,3},{5,4},{6,5},{7,6},{8,7},{9,8},{10,9},{11,1... | collective-permute-start | bytes 4718600 | tf_op jit(solution)/shard_map/ppermute | solution.py:10
  10.0 86.5 %collective-permute-start.1 = (bf16[1024,768]{1,0:T(8,128)(2,1)S(1)}, bf16[1024,768]{1,0:T(8,128)(2,1)S(1)}, u32[]{:S(2)}, u32[]{:S(2)}) collective-permute-start(bf16[1024,768]{1,0:T(8,128)(2,1)S(1)} %fusion.16), channel_id=1, source_target_pairs={{0,1},{1,2},{2,3},{3,4},{4,5},{5,6},{6,7},{7,8},{8,9},{9,10},{10,1... | collective-permute-start | bytes 4718600 | tf_op jit(solution)/shard_map/ppermute | solution.py:10
  43.7 54.9 %collective-permute-start.2 = (bf16[1024,768]{1,0:T(8,128)(2,1)}, bf16[1024,768]{1,0:T(8,128)(2,1)}, u32[]{:S(2)}, u32[]{:S(2)}) collective-permute-start(bf16[1024,768]{1,0:T(8,128)(2,1)} %collective-permute-done), channel_id=1, source_target_pairs={{1,0},{2,1},{3,2},{4,3},{5,4},{6,5},{7,6},{8,7},{9,8},{10,9},{11,1... | collective-permute-start | bytes 4718600 | tf_op jit(solution)/shard_map/ppermute | solution.py:10
  96.5 35.5 %collective-permute-start.4 = (bf16[1024,768]{1,0:T(8,128)(2,1)S(1)}, bf16[1024,768]{1,0:T(8,128)(2,1)S(1)}, u32[]{:S(2)}, u32[]{:S(2)}) collective-permute-start(bf16[1024,768]{1,0:T(8,128)(2,1)S(1)} %collective-permute-done.1), channel_id=1, source_target_pairs={{0,1},{1,2},{2,3},{3,4},{4,5},{5,6},{6,7},{7,8},{8,9},{9,10},{10,1... | collective-permute-start | bytes 4718600 | tf_op jit(solution)/shard_map/ppermute | solution.py:10
  98.6 38.5 %collective-permute-start.5 = (bf16[1024,768]{1,0:T(8,128)(2,1)}, bf16[1024,768]{1,0:T(8,128)(2,1)S(1)}, u32[]{:S(2)}, u32[]{:S(2)}) collective-permute-start(bf16[1024,768]{1,0:T(8,128)(2,1)} %collective-permute-done.2), channel_id=1, source_target_pairs={{1,0},{2,1},{3,2},{4,3},{5,4},{6,5},{7,6},{8,7},{9,8},{10,9},{11,1... | collective-permute-start | bytes 4718600 | tf_op jit(solution)/shard_map/ppermute | solution.py:10
  131.9 34.6 %collective-permute-start.7 = (bf16[1024,768]{1,0:T(8,128)(2,1)S(1)}, bf16[1024,768]{1,0:T(8,128)(2,1)S(1)}, u32[]{:S(2)}, u32[]{:S(2)}) collective-permute-start(bf16[1024,768]{1,0:T(8,128)(2,1)S(1)} %collective-permute-done.4), channel_id=1, source_target_pairs={{0,1},{1,2},{2,3},{3,4},{4,5},{5,6},{6,7},{7,8},{8,9},{9,10},{10,1... | collective-permute-start | bytes 4718600 | tf_op jit(solution)/shard_map/ppermute | solution.py:10
  137.1 33.9 %collective-permute-start.8 = (bf16[1024,768]{1,0:T(8,128)(2,1)S(1)}, bf16[1024,768]{1,0:T(8,128)(2,1)S(1)}, u32[]{:S(2)}, u32[]{:S(2)}) collective-permute-start(bf16[1024,768]{1,0:T(8,128)(2,1)S(1)} %collective-permute-done.5), channel_id=1, source_target_pairs={{1,0},{2,1},{3,2},{4,3},{5,4},{6,5},{7,6},{8,7},{9,8},{10,9},{11,1... | collective-permute-start | bytes 4718600 | tf_op jit(solution)/shard_map/ppermute | solution.py:10
  179.7 25.2 %collective-permute-start.9 = (f32[1024]{0:T(1024)S(1)}, f32[1024]{0:T(1024)S(1)}, u32[]{:S(2)}, u32[]{:S(2)}) collective-permute-start(f32[1024]{0:T(1024)S(1)} %max.76), channel_id=1, source_target_pairs={{3,0},{4,1},{5,2},{6,3},{7,4},{8,5},{9,6},{10,7},{11,8},{12,9},{13... | collective-permute-start | bytes 12296 | tf_op jit(solution)/shard_map/ppermute | solution.py:10
  181.6 25.2 %collective-permute-start.12 = (f32[1024]{0:T(1024)S(1)}, f32[1024]{0:T(1024)S(1)}, u32[]{:S(2)}, u32[]{:S(2)}) collective-permute-start(f32[1024]{0:T(1024)S(1)} %max.82), channel_id=1, source_target_pairs={{0,3},{1,4},{2,5},{3,6},{4,7},{5,8},{6,9},{7,10},{8,11},{9,12},{10... | collective-permute-start | bytes 12296 | tf_op jit(solution)/shard_map/ppermute | solution.py:10
  187.4 23.5 %collective-permute-start.6 = (f32[1024]{0:T(1024)S(1)}, f32[1024]{0:T(1024)S(1)}, u32[]{:S(2)}, u32[]{:S(2)}) collective-permute-start(f32[1024]{0:T(1024)S(1)} %max.72), channel_id=1, source_target_pairs={{2,0},{3,1},{4,2},{5,3},{6,4},{7,5},{8,6},{9,7},{10,8},{11,9},{12,... | collective-permute-start | bytes 12296 | tf_op jit(solution)/shard_map/ppermute | solution.py:10
  193.6 17.2 %collective-permute-start.11 = (f32[1024]{0:T(1024)S(1)}, f32[1024]{0:T(1024)S(1)}, u32[]{:S(2)}, u32[]{:S(2)}) collective-permute-start(f32[1024]{0:T(1024)S(1)} %max.80), channel_id=1, source_target_pairs={{0,2},{1,3},{2,4},{3,5},{4,6},{5,7},{6,8},{7,9},{8,10},{9,11},{10,... | collective-permute-start | bytes 12296 | tf_op jit(solution)/shard_map/ppermute | solution.py:10
  195.6 15.3 %collective-permute-start.3 = (f32[1024]{0:T(1024)S(1)}, f32[1024]{0:T(1024)S(1)}, u32[]{:S(2)}, u32[]{:S(2)}) collective-permute-start(f32[1024]{0:T(1024)S(1)} %max.68), channel_id=1, source_target_pairs={{1,0},{2,1},{3,2},{4,3},{5,4},{6,5},{7,6},{8,7},{9,8},{10,9},{11,1... | collective-permute-start | bytes 12296 | tf_op jit(solution)/shard_map/ppermute | solution.py:10
  204.9 7.6 %collective-permute-start.10 = (f32[1024]{0:T(1024)S(1)}, f32[1024]{0:T(1024)S(1)}, u32[]{:S(2)}, u32[]{:S(2)}) collective-permute-start(f32[1024]{0:T(1024)S(1)} %max.78), channel_id=1, source_target_pairs={{0,1},{1,2},{2,3},{3,4},{4,5},{5,6},{6,7},{7,8},{8,9},{9,10},{10,1... | collective-permute-start | bytes 12296 | tf_op jit(solution)/shard_map/ppermute | solution.py:10
  206.8 10.3 %collective-permute-start.13 = (f32[1024]{0:T(1024)S(1)}, f32[1024]{0:T(1024)S(1)}, u32[]{:S(2)}, u32[]{:S(2)}) collective-permute-start(f32[1024]{0:T(1024)S(1)} %get-tuple-element.29), channel_id=1, source_target_pairs={{0,4},{1,5},{2,6},{3,7},{4,8},{5,9},{6,10},{7,11},{8,12},{9,13},{1... | collective-permute-start | bytes 12296 | tf_op jit(solution)/shard_map/ppermute | solution.py:10

commit v2 on v1

--- a/solution.py
+++ b/solution.py
@@ -23,20 +23,8 @@
     count = lax.axis_size("dev")
     reach = count // 4
     place = lax.axis_index("dev")
+    first_block = (lax.axis_index("group") * count + place) * blocks
     unit = unit_rows(embeddings)
-    all_tags = lax.all_gather(cluster_ids, "dev", tiled=True) + 1
-
-    def tags_at(offset, sentinel):
-        index = place + offset
-        valid = (index >= 0) & (index < count)
-        start = jnp.clip(index, 0, count - 1) * blocks
-        tags = lax.dynamic_slice_in_dim(all_tags, start, blocks, 0)
-        return jnp.repeat(jnp.where(valid, tags, sentinel), width)
-
-    def tile(a, a_tags, b, b_tags):
-        sims = jnp.dot(a, b.T, preferred_element_type=jnp.float32)
-        shifted = jnp.where(a_tags[:, None] == b_tags[None, :], sims + 2.0, jnp.zeros_like(sims))
-        return jnp.max(shifted, axis=1), jnp.max(shifted, axis=0)
 
     own_tags = jnp.repeat(cluster_ids + 1, width)
     local = jnp.arange(rows, dtype=jnp.int32)
@@ -52,14 +40,32 @@
     behind = [unit]
     for step in range(behind_steps):
         behind.append(from_behind(behind[-1], "dev", 1))
-    ahead_tags = [own_tags] + [tags_at(j, -2) for j in range(1, ahead_steps + 1)]
-    behind_tags = [own_tags] + [tags_at(-i, -1) for i in range(1, behind_steps + 1)]
+    ahead_ids = [cluster_ids] + [from_behind(cluster_ids, "dev", -j) for j in range(1, ahead_steps + 1)]
+
+    def tile(i, j):
+        a, b = behind[i], ahead[j]
+        a_blocks = first_block - i * blocks + jnp.arange(blocks, dtype=jnp.int32)
+        valid = place + j < count
+        block_same = (ahead_ids[j][None, :] <= a_blocks[:, None]) & valid
+        matched = jnp.any(block_same)
+
+        def compute(unused):
+            sims = jnp.dot(a, b.T, preferred_element_type=jnp.float32)
+            same = jnp.repeat(jnp.repeat(block_same, width, axis=0), width, axis=1)
+            shifted = jnp.where(same, sims + 2.0, jnp.zeros_like(sims))
+            return jnp.max(shifted, axis=1), jnp.max(shifted, axis=0)
+
+        def skipped(unused):
+            empty = jnp.zeros((rows,), jnp.float32)
+            return (empty, empty)
+
+        return lax.cond(matched, compute, skipped, 0)
 
     to_ahead = [None] * (ahead_steps + 1)
     to_behind = [None] * (behind_steps + 1)
     for k in range(1, reach):
         i, j = k // 2, k - k // 2
-        row_part, column_part = tile(behind[i], behind_tags[i], ahead[j], ahead_tags[j])
+        row_part, column_part = tile(i, j)
         if i == 0:
             best = jnp.maximum(best, row_part)
         else:

time: 219 us -> 258 us (1.18)
  waiting for transfers between devices: 73.6 us -> 124 us
  starting transfers between devices: 61.1 us -> 110 us
  blocking collectives: 44.7 us -> 0 us
  matrix products: 33.2 us -> 6.3 us
  local copies, waits for them, and re-layouts: 1.22 us -> 7.68 us
  between operations: 1.01 us -> 4.96 us
    ppermute x14 -> x18, waiting for transfers between devices: 73.6 us -> 124 us  [from_behind(): lax.ppermute(value, axis, [(source, source + steps) for source in range(i...]
    ppermute x14 -> x18, starting transfers between devices: 61.1 us -> 110 us  [from_behind(): lax.ppermute(value, axis, [(source, source + steps) for source in range(i...]
    unnamed x1 -> x0, blocking collectives: 44.7 us -> none
    dot_general x7 -> x2, matrix products: 31.1 us -> 4.25 us  [compute(): sims = jnp.dot(a, b.T, preferred_element_type=jnp.float32)]
    broadcast_in_dim x0 -> x4, local copies, waits for them, and re-layouts: none -> 6.48 us  [compute(): same = jnp.repeat(jnp.repeat(block_same, width, axis=0), width, axis=1)]
  transfers between devices with their start and end apart: 14 -> 18, of which waited for: 6 -> 6; matrix products, arithmetic and copies ran while one was open for 12% -> 6% of each run, Pallas kernels for 0% -> 0%
where the time goes in v2:
time: 258 us; the launch traced here: 257 us
  waiting for transfers between devices  124 us (48%)
  starting transfers between devices  110 us (43%)
  local copies, waits for them, and re-layouts  7.68 us (3%)
  matrix products  6.3 us (2%)
  between operations  4.96 us (2%)
  other arithmetic  3.75 us (1%)
    ppermute x18, waiting for transfers between devices, from_behind(): lax.ppermute(value, axis, [(source, source + steps) for source in range(i...  124 us
    ppermute x18, starting transfers between devices, from_behind(): lax.ppermute(value, axis, [(source, source + steps) for source in range(i...  110 us
    broadcast_in_dim x4, local copies, waits for them, and re-layouts, compute(): same = jnp.repeat(jnp.repeat(block_same, width, axis=0), width, axis=1)  6.48 us
  transfers between devices with their start and end apart: 18, of which 6 were waited for; matrix products, arithmetic and copies ran while one was open for 6% of the time, Pallas kernels for 0%

profile of v2, /device:TPU:4, one launch (start us, length us, event | category | flops | bytes accessed | tf_op | source)
XLA Modules:
  0.0 257.1 jit_solution(14674170169661210559)
XLA Ops:
  0.0 1.9 fusion.15
  1.9 0.0 copy-start.10
  1.9 0.3 fusion.16
  2.3 7.7 %collective-permute-start.1 = (bf16[1024,768]{1,0:T(8,128)(2,1)S(1)}, bf16[1024,768]{1,0:T(8,128)(2,1)S(1)}, u32[]{:S(2)}, u32[]{:S(2)}) collective-permute-start(bf16[1024,768]{1,0:T(8,128)(2,1)S(1)} %fusion.16), channel_id=1, source_target_pairs={{1,0},{2,1},{3,2},{4,3},{5,4},{6,5},{7,6},{8,7},{9,8},{10,9},{11,1... | collective-permute-start | bytes 4718600 | tf_op jit(solution)/shard_map/ppermute | solution.py:10
  10.0 1.9 collective-permute-start.2
  11.9 31.7 %collective-permute-done.1 = bf16[1024,768]{1,0:T(8,128)(2,1)S(1)} collective-permute-done((bf16[1024,768]{1,0:T(8,128)(2,1)S(1)}, bf16[1024,768]{1,0:T(8,128)(2,1)S(1)}, u32[]{:S(2)}, u32[]{:S(2)}) %collective-permute-start.1) | collective-permute-done | bytes 1572896 | tf_op jit(solution)/shard_map/ppermute | solution.py:10
  43.6 6.5 %collective-permute-start.4 = (bf16[1024,768]{1,0:T(8,128)(2,1)S(1)}, bf16[1024,768]{1,0:T(8,128)(2,1)S(1)}, u32[]{:S(2)}, u32[]{:S(2)}) collective-permute-start(bf16[1024,768]{1,0:T(8,128)(2,1)S(1)} %collective-permute-done.1), channel_id=1, source_target_pairs={{1,0},{2,1},{3,2},{4,3},{5,4},{6,5},{7,6},{8,7},{9,8},{10,9},{11,1... | collective-permute-start | bytes 4718600 | tf_op jit(solution)/shard_map/ppermute | solution.py:10
  50.1 0.0 collective-permute-done.2
  50.2 1.9 collective-permute-start.6
  52.1 30.8 %collective-permute-done.4 = bf16[1024,768]{1,0:T(8,128)(2,1)S(1)} collective-permute-done((bf16[1024,768]{1,0:T(8,128)(2,1)S(1)}, bf16[1024,768]{1,0:T(8,128)(2,1)S(1)}, u32[]{:S(2)}, u32[]{:S(2)}) %collective-permute-start.4) | collective-permute-done | bytes 1572896 | tf_op jit(solution)/shard_map/ppermute | solution.py:10
  82.9 6.5 %collective-permute-start.8 = (bf16[1024,768]{1,0:T(8,128)(2,1)S(1)}, bf16[1024,768]{1,0:T(8,128)(2,1)}, u32[]{:S(2)}, u32[]{:S(2)}) collective-permute-start(bf16[1024,768]{1,0:T(8,128)(2,1)S(1)} %collective-permute-done.4), channel_id=1, source_target_pairs={{1,0},{2,1},{3,2},{4,3},{5,4},{6,5},{7,6},{8,7},{9,8},{10,9},{11,1... | collective-permute-start | bytes 4718600 | tf_op jit(solution)/shard_map/ppermute | solution.py:10
  89.4 0.0 collective-permute-done.6
  89.4 1.9 collective-permute-start.10
  91.4 30.0 %collective-permute-done.8 = bf16[1024,768]{1,0:T(8,128)(2,1)} collective-permute-done((bf16[1024,768]{1,0:T(8,128)(2,1)S(1)}, bf16[1024,768]{1,0:T(8,128)(2,1)}, u32[]{:S(2)}, u32[]{:S(2)}) %collective-permute-start.8) | collective-permute-done | bytes 1572896 | tf_op jit(solution)/shard_map/ppermute | solution.py:10
  121.3 6.6 %collective-permute-start.12 = (bf16[1024,768]{1,0:T(8,128)(2,1)}, bf16[1024,768]{1,0:T(8,128)(2,1)}, u32[]{:S(2)}, u32[]{:S(2)}) collective-permute-start(bf16[1024,768]{1,0:T(8,128)(2,1)} %collective-permute-done.8), channel_id=1, source_target_pairs={{1,0},{2,1},{3,2},{4,3},{5,4},{6,5},{7,6},{8,7},{9,8},{10,9},{11,1... | collective-permute-start | bytes 4718600 | tf_op jit(solution)/shard_map/ppermute | solution.py:10
  127.9 1.9 collective-permute-start.3
  129.9 1.9 collective-permute-start
  131.8 4.2 %collective-permute-start.11 = (s32[4]{0:T(128)S(1)}, s32[4]{0:T(128)S(1)}, u32[]{:S(2)}, u32[]{:S(2)}) collective-permute-start(s32[4]{0:T(128)S(1)} %copy-done.10), channel_id=1, source_target_pairs={{4,0},{5,1},{6,2},{7,3},{8,4},{9,5},{10,6},{11,7},{12,8},{13,9},{1... | collective-permute-start | bytes 56 | tf_op jit(solution)/shard_map/ppermute | solution.py:10
  136.1 23.3 %collective-permute-done.3 = s32[4]{0:T(128)S(1)} collective-permute-done((s32[4]{0:T(128)S(1)}, s32[4]{0:T(128)S(1)}, u32[]{:S(2)}, u32[]{:S(2)}) %collective-permute-start.3) | collective-permute-done | bytes 48 | tf_op jit(solution)/shard_map/ppermute | solution.py:10
  159.4 4.9 %collective-permute-start.7 = (s32[4]{0:T(128)S(1)}, s32[4]{0:T(128)S(1)}, u32[]{:S(2)}, u32[]{:S(2)}) collective-permute-start(s32[4]{0:T(128)S(1)} %copy-done.10), channel_id=1, source_target_pairs={{3,0},{4,1},{5,2},{6,3},{7,4},{8,5},{9,6},{10,7},{11,8},{12,9},{13... | collective-permute-start | bytes 56 | tf_op jit(solution)/shard_map/ppermute | solution.py:10
  164.3 0.0 collective-permute-done.11
  164.3 2.3 collective-permute-done.7
  166.6 0.9 fusion.17
  170.1 6.0 %conditional.7 = (f32[1024]{0:T(1024)S(1)}, f32[1024]{0:T(1024)S(1)}) conditional(s32[]{:T(128)} %convert_element_type.29, () %tuple.61, (pred[4,4]{1,0:T(4,128)(4,1)S(1)}, bf16[1024,768]{1,0:T(8,128)(2,1)S(1)}, bf16[1024,768]{1,0:T(8,128)(2,1)}) %tuple.121), branch_computations={%region_3.4_spmd, %region_4.7_spmd} | conditional | flops 1614804992 | bytes 13647932 | solution.py:62
  170.1 3.2 %broadcast_in_dim.10 = pred[1024,4,256]{2,1,0:T(4,128)(4,1)S(1)} broadcast(pred[1024,4]{1,0:T(8,128)(4,1)S(1)} %bitcast.54), dimensions={0,1} | broadcast | bytes 1052672 | tf_op jit(solution)/shard_map/cond/branch_1_fun/broadcast_in_dim | solution.py:54
  173.3 0.5 copy.3
  173.9 2.1 fusion
  176.0 6.0 %conditional.8 = (f32[1024]{0:T(1024)S(1)}, f32[1024]{0:T(1024)S(1)}) conditional(s32[]{:T(128)} %convert_element_type.30, () %tuple.63, (pred[4,4]{1,0:T(4,128)(4,1)S(1)}, bf16[1024,768]{1,0:T(8,128)(2,1)}, bf16[1024,768]{1,0:T(8,128)(2,1)}) %tuple.122), branch_computations={%region_8.9_spmd, %region_9.12_spmd} | conditional | flops 1614804992 | bytes 19939416 | solution.py:62
  176.1 3.2 %broadcast_in_dim.17 = pred[1024,4,256]{2,1,0:T(4,128)(4,1)S(1)} broadcast(pred[1024,4]{1,0:T(8,128)(4,1)S(1)} %bitcast.55), dimensions={0,1} | broadcast | bytes 1052672 | tf_op jit(solution)/shard_map/cond/branch_1_fun/broadcast_in_dim | solution.py:54
  179.3 0.5 copy.4
  179.9 2.1 fusion.2
  182.0 1.9 collective-permute-start.14
  184.0 0.2 conditional.10
  184.2 12.4 %collective-permute-start.15 = (f32[1024]{0:T(1024)S(1)}, f32[1024]{0:T(1024)S(1)}, u32[]{:S(2)}, u32[]{:S(2)}) collective-permute-start(f32[1024]{0:T(1024)S(1)} %max.51), channel_id=1, source_target_pairs={{0,2},{1,3},{2,4},{3,5},{4,6},{5,7},{6,8},{7,9},{8,10},{9,11},{10,... | collective-permute-start | bytes 12296 | tf_op jit(solution)/shard_map/ppermute | solution.py:10
  196.6 0.1 broadcast_bitcast_fusion
  198.6 8.8 %collective-permute-start.5 = (f32[1024]{0:T(1024)S(1)}, f32[1024]{0:T(1024)S(1)}, u32[]{:S(2)}, u32[]{:S(2)}) collective-permute-start(f32[1024]{0:T(1024)S(1)} %max.43), channel_id=1, source_target_pairs={{1,0},{2,1},{3,2},{4,3},{5,4},{6,5},{7,6},{8,7},{9,8},{10,9},{11,1... | collective-permute-start | bytes 12296 | tf_op jit(solution)/shard_map/ppermute | solution.py:10
  207.5 0.0 collective-permute-done.10
  207.6 14.1 %collective-permute-start.16 = (f32[1024]{0:T(1024)S(1)}, f32[1024]{0:T(1024)S(1)}, u32[]{:S(2)}, u32[]{:S(2)}) collective-permute-start(f32[1024]{0:T(1024)S(1)} %max.53), channel_id=1, source_target_pairs={{0,3},{1,4},{2,5},{3,6},{4,7},{5,8},{6,9},{7,10},{8,11},{9,12},{10... | collective-permute-start | bytes 12296 | tf_op jit(solution)/shard_map/ppermute | solution.py:10
  221.8 10.1 %collective-permute-start.9 = (f32[1024]{0:T(1024)S(1)}, f32[1024]{0:T(1024)S(1)}, u32[]{:S(2)}, u32[]{:S(2)}) collective-permute-start(f32[1024]{0:T(1024)S(1)} %max.45), channel_id=1, source_target_pairs={{2,0},{3,1},{4,2},{5,3},{6,4},{7,5},{8,6},{9,7},{10,8},{11,9},{12,... | collective-permute-start | bytes 12296 | tf_op jit(solution)/shard_map/ppermute | solution.py:10
  232.0 0.0 collective-permute-done.14
  232.0 14.2 %collective-permute-start.13 = (f32[1024]{0:T(1024)S(1)}, f32[1024]{0:T(1024)S(1)}, u32[]{:S(2)}, u32[]{:S(2)}) collective-permute-start(f32[1024]{0:T(1024)S(1)} %max.47), channel_id=1, source_target_pairs={{3,0},{4,1},{5,2},{6,3},{7,4},{8,5},{9,6},{10,7},{11,8},{12,9},{13... | collective-permute-start | bytes 12296 | tf_op jit(solution)/shard_map/ppermute | solution.py:10
  246.2 0.0 collective-permute-done.15
  246.2 1.9 collective-permute-start.17
  248.2 2.1 select_reduce_fusion
  250.2 0.0 collective-permute-done.5
  250.2 0.0 collective-permute-done.16
  250.3 6.3 %collective-permute-done.17 = f32[1024]{0:T(1024)S(1)} collective-permute-done((f32[1024]{0:T(1024)S(1)}, f32[1024]{0:T(1024)S(1)}, u32[]{:S(2)}, u32[]{:S(2)}) %collective-permute-start.17) | collective-permute-done | bytes 4128 | tf_op jit(solution)/shard_map/ppermute | solution.py:10
  256.5 0.6 maximum_add_fusion
  (46 shorter events, 0.3 us)
Async XLA Ops:
  0.0 1.9 copy-start
  1.9 126.0 %copy-start.10 = (s32[4]{0:T(128)S(1)}, s32[4]{0:T(128)}, u32[]{:S(2)}) copy-start(s32[4]{0:T(128)} %param.17) | copy-start | bytes 52
  2.3 41.4 %collective-permute-start.1 = (bf16[1024,768]{1,0:T(8,128)(2,1)S(1)}, bf16[1024,768]{1,0:T(8,128)(2,1)S(1)}, u32[]{:S(2)}, u32[]{:S(2)}) collective-permute-start(bf16[1024,768]{1,0:T(8,128)(2,1)S(1)} %fusion.16), channel_id=1, source_target_pairs={{1,0},{2,1},{3,2},{4,3},{5,4},{6,5},{7,6},{8,7},{9,8},{10,9},{11,1... | collective-permute-start | bytes 4718600 | tf_op jit(solution)/shard_map/ppermute | solution.py:10
  10.0 40.1 %collective-permute-start.2 = (bf16[1024,768]{1,0:T(8,128)(2,1)S(1)}, bf16[1024,768]{1,0:T(8,128)(2,1)S(1)}, u32[]{:S(2)}, u32[]{:S(2)}) collective-permute-start(bf16[1024,768]{1,0:T(8,128)(2,1)S(1)} %fusion.16), channel_id=1, source_target_pairs={{0,1},{1,2},{2,3},{3,4},{4,5},{5,6},{6,7},{7,8},{8,9},{9,10},{10,1... | collective-permute-start | bytes 4718600 | tf_op jit(solution)/shard_map/ppermute | solution.py:10
  43.6 88.2 %copy-start.7 = (bf16[1024,768]{1,0:T(8,128)(2,1)}, bf16[1024,768]{1,0:T(8,128)(2,1)S(1)}, u32[]{:S(2)}) copy-start(bf16[1024,768]{1,0:T(8,128)(2,1)S(1)} %collective-permute-done.1) | copy-start | bytes 4718596
  43.6 39.3 %collective-permute-start.4 = (bf16[1024,768]{1,0:T(8,128)(2,1)S(1)}, bf16[1024,768]{1,0:T(8,128)(2,1)S(1)}, u32[]{:S(2)}, u32[]{:S(2)}) collective-permute-start(bf16[1024,768]{1,0:T(8,128)(2,1)S(1)} %collective-permute-done.1), channel_id=1, source_target_pairs={{1,0},{2,1},{3,2},{4,3},{5,4},{6,5},{7,6},{8,7},{9,8},{10,9},{11,1... | collective-permute-start | bytes 4718600 | tf_op jit(solution)/shard_map/ppermute | solution.py:10
  50.2 39.3 %copy-start.4 = (bf16[1024,768]{1,0:T(8,128)(2,1)}, bf16[1024,768]{1,0:T(8,128)(2,1)S(1)}, u32[]{:S(2)}) copy-start(bf16[1024,768]{1,0:T(8,128)(2,1)S(1)} %collective-permute-done.2) | copy-start | bytes 4718596
  50.2 39.3 %collective-permute-start.6 = (bf16[1024,768]{1,0:T(8,128)(2,1)S(1)}, bf16[1024,768]{1,0:T(8,128)(2,1)}, u32[]{:S(2)}, u32[]{:S(2)}) collective-permute-start(bf16[1024,768]{1,0:T(8,128)(2,1)S(1)} %collective-permute-done.2), channel_id=1, source_target_pairs={{0,1},{1,2},{2,3},{3,4},{4,5},{5,6},{6,7},{7,8},{8,9},{9,10},{10,1... | collective-permute-start | bytes 4718600 | tf_op jit(solution)/shard_map/ppermute | solution.py:10
  82.9 47.0 %copy-start.1 = (bf16[1024,768]{1,0:T(8,128)(2,1)}, bf16[1024,768]{1,0:T(8,128)(2,1)S(1)}, u32[]{:S(2)}) copy-start(bf16[1024,768]{1,0:T(8,128)(2,1)S(1)} %collective-permute-done.4) | copy-start | bytes 4718596
  82.9 38.4 %collective-permute-start.8 = (bf16[1024,768]{1,0:T(8,128)(2,1)S(1)}, bf16[1024,768]{1,0:T(8,128)(2,1)}, u32[]{:S(2)}, u32[]{:S(2)}) collective-permute-start(bf16[1024,768]{1,0:T(8,128)(2,1)S(1)} %collective-permute-done.4), channel_id=1, source_target_pairs={{1,0},{2,1},{3,2},{4,3},{5,4},{6,5},{7,6},{8,7},{9,8},{10,9},{11,1... | collective-permute-start | bytes 4718600 | tf_op jit(solution)/shard_map/ppermute | solution.py:10
  89.4 118.1 %collective-permute-start.10 = (bf16[1024,768]{1,0:T(8,128)(2,1)}, bf16[1024,768]{1,0:T(8,128)(2,1)S(1)}, u32[]{:S(2)}, u32[]{:S(2)}) collective-permute-start(bf16[1024,768]{1,0:T(8,128)(2,1)} %collective-permute-done.6), channel_id=1, source_target_pairs={{0,1},{1,2},{2,3},{3,4},{4,5},{5,6},{6,7},{7,8},{8,9},{9,10},{10,1... | collective-permute-start | bytes 4718600 | tf_op jit(solution)/shard_map/ppermute | solution.py:10
  121.3 100.4 %collective-permute-start.12 = (bf16[1024,768]{1,0:T(8,128)(2,1)}, bf16[1024,768]{1,0:T(8,128)(2,1)}, u32[]{:S(2)}, u32[]{:S(2)}) collective-permute-start(bf16[1024,768]{1,0:T(8,128)(2,1)} %collective-permute-done.8), channel_id=1, source_target_pairs={{1,0},{2,1},{3,2},{4,3},{5,4},{6,5},{7,6},{8,7},{9,8},{10,9},{11,1... | collective-permute-start | bytes 4718600 | tf_op jit(solution)/shard_map/ppermute | solution.py:10
  127.9 31.4 %collective-permute-start.3 = (s32[4]{0:T(128)S(1)}, s32[4]{0:T(128)S(1)}, u32[]{:S(2)}, u32[]{:S(2)}) collective-permute-start(s32[4]{0:T(128)S(1)} %copy-done.10), channel_id=1, source_target_pairs={{2,0},{3,1},{4,2},{5,3},{6,4},{7,5},{8,6},{9,7},{10,8},{11,9},{12,... | collective-permute-start | bytes 56 | tf_op jit(solution)/shard_map/ppermute | solution.py:10
  129.9 34.4 %collective-permute-start = (s32[4]{0:T(128)S(1)}, s32[4]{0:T(128)S(1)}, u32[]{:S(2)}, u32[]{:S(2)}) collective-permute-start(s32[4]{0:T(128)S(1)} %copy-done.10), channel_id=1, source_target_pairs={{1,0},{2,1},{3,2},{4,3},{5,4},{6,5},{7,6},{8,7},{9,8},{10,9},{11,1... | collective-permute-start | bytes 56 | tf_op jit(solution)/shard_map/ppermute | solution.py:10
  131.8 32.5 %collective-permute-start.11 = (s32[4]{0:T(128)S(1)}, s32[4]{0:T(128)S(1)}, u32[]{:S(2)}, u32[]{:S(2)}) collective-permute-start(s32[4]{0:T(128)S(1)} %copy-done.10), channel_id=1, source_target_pairs={{4,0},{5,1},{6,2},{7,3},{8,4},{9,5},{10,6},{11,7},{12,8},{13,9},{1... | collective-permute-start | bytes 56 | tf_op jit(solution)/shard_map/ppermute | solution.py:10
  159.4 7.2 %collective-permute-start.7 = (s32[4]{0:T(128)S(1)}, s32[4]{0:T(128)S(1)}, u32[]{:S(2)}, u32[]{:S(2)}) collective-permute-start(s32[4]{0:T(128)S(1)} %copy-done.10), channel_id=1, source_target_pairs={{3,0},{4,1},{5,2},{6,3},{7,4},{8,5},{9,6},{10,7},{11,8},{12,9},{13... | collective-permute-start | bytes 56 | tf_op jit(solution)/shard_map/ppermute | solution.py:10
  170.1 3.8 %copy-start.8 = (bf16[1024,768]{1,0:T(8,128)(2,1)S(1)}, bf16[1024,768]{1,0:T(8,128)(2,1)}, u32[]{:S(2)}) copy-start(bf16[1024,768]{1,0:T(8,128)(2,1)} %get-tuple-element.49) | copy-start | bytes 4718596 | tf_op jit(solution)/shard_map/cond
  176.1 3.8 %copy-start.5 = (bf16[1024,768]{1,0:T(8,128)(2,1)S(1)}, bf16[1024,768]{1,0:T(8,128)(2,1)}, u32[]{:S(2)}) copy-start(bf16[1024,768]{1,0:T(8,128)(2,1)} %get-tuple-element.51) | copy-start | bytes 4718596 | tf_op jit(solution)/shard_map/cond
  176.1 3.8 %copy-start.9 = (bf16[1024,768]{1,0:T(8,128)(2,1)S(1)}, bf16[1024,768]{1,0:T(8,128)(2,1)}, u32[]{:S(2)}) copy-start(bf16[1024,768]{1,0:T(8,128)(2,1)} %get-tuple-element.52) | copy-start | bytes 4718596 | tf_op jit(solution)/shard_map/cond
  182.0 50.0 %collective-permute-start.14 = (f32[1024]{0:T(1024)S(1)}, f32[1024]{0:T(1024)S(1)}, u32[]{:S(2)}, u32[]{:S(2)}) collective-permute-start(f32[1024]{0:T(1024)S(1)} %max.49), channel_id=1, source_target_pairs={{0,1},{1,2},{2,3},{3,4},{4,5},{5,6},{6,7},{7,8},{8,9},{9,10},{10,1... | collective-permute-start | bytes 12296 | tf_op jit(solution)/shard_map/ppermute | solution.py:10
  184.2 62.0 %collective-permute-start.15 = (f32[1024]{0:T(1024)S(1)}, f32[1024]{0:T(1024)S(1)}, u32[]{:S(2)}, u32[]{:S(2)}) collective-permute-start(f32[1024]{0:T(1024)S(1)} %max.51), channel_id=1, source_target_pairs={{0,2},{1,3},{2,4},{3,5},{4,6},{5,7},{6,8},{7,9},{8,10},{9,11},{10,... | collective-permute-start | bytes 12296 | tf_op jit(solution)/shard_map/ppermute | solution.py:10
  198.6 51.6 %collective-permute-start.5 = (f32[1024]{0:T(1024)S(1)}, f32[1024]{0:T(1024)S(1)}, u32[]{:S(2)}, u32[]{:S(2)}) collective-permute-start(f32[1024]{0:T(1024)S(1)} %max.43), channel_id=1, source_target_pairs={{1,0},{2,1},{3,2},{4,3},{5,4},{6,5},{7,6},{8,7},{9,8},{10,9},{11,1... | collective-permute-start | bytes 12296 | tf_op jit(solution)/shard_map/ppermute | solution.py:10
  207.6 42.7 %collective-permute-start.16 = (f32[1024]{0:T(1024)S(1)}, f32[1024]{0:T(1024)S(1)}, u32[]{:S(2)}, u32[]{:S(2)}) collective-permute-start(f32[1024]{0:T(1024)S(1)} %max.53), channel_id=1, source_target_pairs={{0,3},{1,4},{2,5},{3,6},{4,7},{5,8},{6,9},{7,10},{8,11},{9,12},{10... | collective-permute-start | bytes 12296 | tf_op jit(solution)/shard_map/ppermute | solution.py:10
  221.8 28.5 %collective-permute-start.9 = (f32[1024]{0:T(1024)S(1)}, f32[1024]{0:T(1024)S(1)}, u32[]{:S(2)}, u32[]{:S(2)}) collective-permute-start(f32[1024]{0:T(1024)S(1)} %max.45), channel_id=1, source_target_pairs={{2,0},{3,1},{4,2},{5,3},{6,4},{7,5},{8,6},{9,7},{10,8},{11,9},{12,... | collective-permute-start | bytes 12296 | tf_op jit(solution)/shard_map/ppermute | solution.py:10
  232.0 18.3 %collective-permute-start.13 = (f32[1024]{0:T(1024)S(1)}, f32[1024]{0:T(1024)S(1)}, u32[]{:S(2)}, u32[]{:S(2)}) collective-permute-start(f32[1024]{0:T(1024)S(1)} %max.47), channel_id=1, source_target_pairs={{3,0},{4,1},{5,2},{6,3},{7,4},{8,5},{9,6},{10,7},{11,8},{12,9},{13... | collective-permute-start | bytes 12296 | tf_op jit(solution)/shard_map/ppermute | solution.py:10
  246.2 10.3 %collective-permute-start.17 = (f32[1024]{0:T(1024)S(1)}, f32[1024]{0:T(1024)S(1)}, u32[]{:S(2)}, u32[]{:S(2)}) collective-permute-start(f32[1024]{0:T(1024)S(1)} %get-tuple-element.95), channel_id=1, source_target_pairs={{0,4},{1,5},{2,6},{3,7},{4,8},{5,9},{6,10},{7,11},{8,12},{9,13},{1... | collective-permute-start | bytes 12296 | tf_op jit(solution)/shard_map/ppermute | solution.py:10
